TPU v7x, 256 devices: a whole 4x4x8 slice. The times are simulated.
256 devices in a mesh: corpus: 32 (over z, x), group: 8 (over y, core).
Axes of the slice: x: 4, y: 4, z: 8, core: 2. Of those that a mesh axis runs over, the one named last changes fastest.
Arguments:
- embeddings: float32 [196608, 768], P(('corpus', 'group')), may hold values from -150 to 150
- labels: int32 [196608, 1], P(('corpus', 'group')), may hold values from 0 to 255, as said below
- neighbours: int32 [256], replicated, may hold values from 0 to 255, as said below
Outputs:
- dup_score: float32 [196608], P(('corpus', 'group'))
- typical: float32 [196608], P(('corpus', 'group'))
Inputs may be any that keep to these rules, and one draw needn't show every extreme that they name: `labels`: in the rows of one device no cluster is named by more than 6 rows, and some cluster by exactly 6; every cluster is named by some row. `neighbours`: each cluster is the neighbour of exactly one cluster, and never its own.
All inputs are finite; a program needn't handle non-finite values.
Results may differ from a plain program's by a relative error of at most 0.0013.
Values may be sent and summed in bfloat16 or wider, within the bound.
No kernel may reach another device: no remote copies, remote signals or barrier semaphores. Data moves between devices by JAX's collectives and lax.ppermute only.
A program may use at most 128 MiB of HBM per device.

v0:
```python
import math
import jax
import jax.numpy as jnp
from jax import lax
from jax.sharding import PartitionSpec as P

MOST = 6
SHARPNESS = 16.0
TYPICAL_SCALE = 8.0
EPSILON = 1e-06


def normalize(values):
    return values * lax.rsqrt(jnp.sum(values * values, axis=-1, keepdims=True) + EPSILON)


def lookup(lookup_table, positions):
    table_ids = jnp.arange(lookup_table.shape[0], dtype=jnp.int32)
    matches = positions[:, None] == table_ids[None, :]
    return jnp.sum(
        jnp.where(matches, lookup_table[None, :], jnp.zeros_like(lookup_table)[None, :]), axis=1
    )


def fill_slots(unit_embed, positions, slot_total):
    row_ids = jnp.arange(unit_embed.shape[0], dtype=jnp.int32)
    source = jnp.full((slot_total,), -1, jnp.int32).at[positions].set(row_ids)
    present = source >= 0
    picked = jnp.take(unit_embed, jnp.maximum(source, 0), axis=0)
    picked = jnp.where(present[:, None], picked, jnp.zeros_like(picked))
    return (picked, present.astype(jnp.bfloat16))


def pair_sums(block_rows, col_rows, col_mask, distinct):
    similarity = lax.dot_general(
        block_rows, col_rows, (((1,), (1,)), ((), ())), preferred_element_type=jnp.float32
    )
    weights = jnp.exp(SHARPNESS * similarity) * col_mask.astype(jnp.float32)[None, :]
    if distinct is not None:
        weights = jnp.where(distinct, weights, 0.0)
    return jnp.sum(weights, axis=1)


def body(embeddings, labels, neighbours):
    corpus_size = lax.axis_size("corpus")
    group_size = lax.axis_size("group")
    row_count, feature_width = embeddings.shape
    clusters = neighbours.shape[0]
    per_owner = clusters // corpus_size
    per_device = clusters // (corpus_size * group_size)
    slot_total = clusters * MOST
    unit_embed = normalize(embeddings).astype(jnp.bfloat16)
    row_label = labels[:, 0]
    cluster_ids = jnp.arange(clusters, dtype=jnp.int32)
    previous = jnp.sum(
        jnp.where(neighbours[None, :] == cluster_ids[:, None], cluster_ids[None, :], 0), axis=1
    )
    row_ids = jnp.arange(row_count, dtype=jnp.int32)
    before = (row_label[None, :] == row_label[:, None]) & (row_ids[None, :] < row_ids[:, None])
    row_slot = jnp.sum(before.astype(jnp.int32), axis=1)
    near_label = lookup(previous, row_label)
    own_owner = row_label // per_owner
    own_rank = row_label % per_owner
    near_owner = near_label // per_owner
    near_rank = near_label % per_owner
    corpus_at = lax.axis_index("corpus")
    group_at = lax.axis_index("group")
    member_hot = (row_label[:, None] == cluster_ids[None, :]).astype(jnp.bfloat16)
    cluster_sums = lax.dot_general(
        member_hot, unit_embed, (((0,), (0,)), ((), ())), preferred_element_type=jnp.float32
    )
    local_counts = jnp.sum(member_hot, axis=0, dtype=jnp.float32)
    cluster_sums, counts = lax.psum((cluster_sums, local_counts), ("corpus", "group"))
    centroid = normalize(cluster_sums)
    typical_rows = TYPICAL_SCALE * jnp.sum(
        unit_embed * jnp.take(centroid, row_label, axis=0), axis=1
    )

    def slot_of(owner_at, rank_at):
        return (
            (owner_at * group_size + rank_at % group_size) * per_device + rank_at // group_size
        ) * MOST + row_slot

    member_buf, member_mask = fill_slots(unit_embed, slot_of(own_owner, own_rank), slot_total)
    near_buf, near_mask = fill_slots(unit_embed, slot_of(near_owner, near_rank), slot_total)
    shape_rows = (corpus_size, group_size, per_device, MOST, feature_width)
    shape_mask = (corpus_size, group_size, per_device, MOST)
    arrived = (
        lax.all_to_all(
            lax.all_to_all(
                member_buf.reshape(shape_rows), "corpus", split_axis=0, concat_axis=3, tiled=True
            ),
            "group",
            split_axis=1,
            concat_axis=3,
            tiled=True,
        ),
        lax.all_to_all(
            lax.all_to_all(
                near_buf.reshape(shape_rows), "corpus", split_axis=0, concat_axis=3, tiled=True
            ),
            "group",
            split_axis=1,
            concat_axis=3,
            tiled=True,
        ),
        lax.all_to_all(
            lax.all_to_all(
                member_mask.reshape(shape_mask), "corpus", split_axis=0, concat_axis=3, tiled=True
            ),
            "group",
            split_axis=1,
            concat_axis=3,
            tiled=True,
        ),
        lax.all_to_all(
            lax.all_to_all(
                near_mask.reshape(shape_mask), "corpus", split_axis=0, concat_axis=3, tiled=True
            ),
            "group",
            split_axis=1,
            concat_axis=3,
            tiled=True,
        ),
    )
    cluster_span = group_size * corpus_size * MOST
    member_rows = arrived[0].reshape(per_device, cluster_span, feature_width)
    other_rows = arrived[1].reshape(per_device, cluster_span, feature_width)
    member_valid = arrived[2].reshape(per_device, cluster_span)
    other_valid = arrived[3].reshape(per_device, cluster_span)
    mine = corpus_at * per_owner + jnp.arange(per_device, dtype=jnp.int32) * group_size + group_at
    own_count = lookup(counts, mine)
    near_count = lookup(counts, lookup(neighbours, mine))
    block_size = math.gcd(cluster_span, 1024)
    col_ids = jnp.arange(cluster_span, dtype=jnp.int32)

    def one_cluster(cluster_item):
        members, others, member_flags, other_flags, count_own, count_near = cluster_item

        def one_block(first_row):
            block_rows = lax.dynamic_slice_in_dim(members, first_row, block_size, 0)
            distinct = (first_row + jnp.arange(block_size, dtype=jnp.int32))[:, None] != col_ids[
                None, :
            ]
            return (
                pair_sums(block_rows, members, member_flags, distinct),
                pair_sums(block_rows, others, other_flags, None),
            )

        own_sum, near_sum = lax.map(
            one_block, jnp.arange(cluster_span // block_size, dtype=jnp.int32) * block_size
        )
        return jnp.log(
            1.0
            + own_sum.reshape(cluster_span) / count_own
            + near_sum.reshape(cluster_span) / count_near
        )

    scores = lax.map(
        one_cluster, (member_rows, other_rows, member_valid, other_valid, own_count, near_count)
    )
    payload = scores[None]
    layers = payload.shape[0]
    payload = payload.reshape(layers, 1, per_device, group_size, corpus_size, MOST)
    returned = lax.all_to_all(
        lax.all_to_all(payload, "corpus", split_axis=4, concat_axis=1, tiled=True),
        "group",
        split_axis=3,
        concat_axis=4,
        tiled=True,
    )
    returned = returned.reshape(layers, slot_total)
    home_slot = (
        (own_owner * per_device + own_rank // group_size) * group_size + own_rank % group_size
    ) * MOST + row_slot
    dup_score = jnp.take(returned[0], home_slot)
    return (dup_score, typical_rows)


def solution(mesh):
    placed = (P(("corpus", "group"), None), P(("corpus", "group"), None), P())
    return jax.shard_map(
        body,
        mesh=mesh,
        in_specs=placed,
        out_specs=(P(("corpus", "group")), P(("corpus", "group"))),
        check_vma=False,
    )
```

profile of v0, /device:TPU:1, one launch (start us, length us, event | category | flops | bytes accessed | tf_op | source)
XLA Modules:
  0.0 593.5 jit_solution(3198293003437910147)
XLA Ops:
  17.5 12.0 %all-to-all-start.6 = ((bf16[32,8,1,6]{3,1,2,0:T(8,128)(2,1)}), bf16[32,8,1,6]{3,1,2,0:T(8,128)(2,1)}, u32[]{:S(2)}, u32[]{:S(2)}) async-start(bf16[32,8,1,6]{3,1,2,0:T(8,128)(2,1)} %bitcast.11), calls=%async_computation.6 | async-start | bytes 131072 | tf_op jit(solution)/shard_map/all_to_all | solution.py:117
  38.3 8.8 %all-to-all-start.2 = ((bf16[32,8,1,6]{3,1,2,0:T(8,128)(2,1)}), bf16[32,8,1,6]{3,1,2,0:T(8,128)(2,1)}, u32[]{:S(2)}, u32[]{:S(2)}) async-start(bf16[32,8,1,6]{3,1,2,0:T(8,128)(2,1)} %bitcast.58), calls=%async_computation.2 | async-start | bytes 131072 | tf_op jit(solution)/shard_map/all_to_all | solution.py:108
  55.9 7.1 %all-to-all-start.7 = ((bf16[1,8,1,192]{3,2,0,1:T(2,128)(2,1)}), bf16[1,8,1,192]{3,2,0,1:T(2,128)(2,1)}, u32[]{:S(2)}, u32[]{:S(2)}) async-start(bf16[1,8,1,192]{3,2,0,1:T(2,128)(2,1)} %all_to_all.126), calls=%async_computation.7 | async-start | bytes 16384 | tf_op jit(solution)/shard_map/all_to_all | solution.py:116
  64.3 5.7 gather_fusion.3
  74.6 4.8 all-to-all-start.3
  82.8 5.0 reshape.320
  87.8 3.9 copy.42
  91.7 5.5 all-to-all-start.4
  97.2 5.7 gather_fusion.2
  106.3 5.0 reshape.317
  111.4 3.9 copy.36
  115.3 35.8 %all-to-all-done.4 = bf16[32,8,1,6,768]{4,1,3,2,0:T(8,128)(2,1)} async-done(((bf16[32,8,1,6,768]{4,1,3,2,0:T(8,128)(2,1)}), bf16[32,8,1,6,768]{4,1,3,2,0:T(8,128)(2,1)}, u32[]{:S(2)}, u32[]{:S(2)}) %all-to-all-start.4) | async-done | bytes 2359328 | tf_op jit(solution)/shard_map/all_to_all | solution.py:99
  151.2 7.6 %all-to-all-start = ((bf16[32,8,1,6,768]{4,1,3,2,0:T(8,128)(2,1)}), bf16[32,8,1,6,768]{4,1,3,2,0:T(8,128)(2,1)}, u32[]{:S(2)}, u32[]{:S(2)}) async-start(bf16[32,8,1,6,768]{4,1,3,2,0:T(8,128)(2,1)} %copy.36), calls=%async_computation | async-start | bytes 4718592 | tf_op jit(solution)/shard_map/all_to_all | solution.py:90
  162.2 50.3 %all-to-all-done = bf16[32,8,1,6,768]{4,1,3,2,0:T(8,128)(2,1)} async-done(((bf16[32,8,1,6,768]{4,1,3,2,0:T(8,128)(2,1)}), bf16[32,8,1,6,768]{4,1,3,2,0:T(8,128)(2,1)}, u32[]{:S(2)}, u32[]{:S(2)}) %all-to-all-start) | async-done | bytes 2359328 | tf_op jit(solution)/shard_map/all_to_all | solution.py:90
  212.5 7.1 %all-to-all-start.5 = ((bf16[1,8,1,192,768]{4,3,2,0,1:T(8,128)(2,1)}), bf16[1,8,1,192,768]{4,3,2,0,1:T(8,128)(2,1)}, u32[]{:S(2)}, u32[]{:S(2)}) async-start(bf16[1,8,1,192,768]{4,3,2,0,1:T(8,128)(2,1)} %copy.43), calls=%async_computation.5 | async-start | bytes 4718592 | tf_op jit(solution)/shard_map/all_to_all | solution.py:98
  223.1 25.8 %all-to-all-done.5 = bf16[1,8,1,192,768]{4,3,2,0,1:T(8,128)(2,1)} async-done(((bf16[1,8,1,192,768]{4,3,2,0,1:T(8,128)(2,1)}), bf16[1,8,1,192,768]{4,3,2,0,1:T(8,128)(2,1)}, u32[]{:S(2)}, u32[]{:S(2)}) %all-to-all-start.5) | async-done | bytes 2359328 | tf_op jit(solution)/shard_map/all_to_all | solution.py:98
  248.9 5.1 all-to-all-start.1
  258.5 91.5 %psum.14 = f32[256]{0:T(256)S(1)} all-reduce(f32[256]{0:T(256)S(1)} %convert_reduce_fusion.1), channel_id=1, replica_groups=mesh['corpus'=32,'group'=8] {'corpus','group'}, use_global_device_ids=true, to_apply=%region_11.13 | all-reduce | flops 256 | bytes 2048 | tf_op jit(solution)/shard_map/psum | solution.py:73
  353.7 161.5 %all-reduce.2.cloned.1.call-done = f32[256,768]{1,0:T(8,128)} async-done(((f32[256,768]{1,0:T(8,128)}), f32[256,768]{1,0:T(8,128)}) %all-reduce.2.cloned.1.call-update) | async-done | bytes 786448 | tf_op jit(solution)/shard_map/psum | solution.py:73
  516.5 31.4 %while.21 = (s32[]{:T(128)}, f32[3,512]{1,0:T(4,128)S(1)}, f32[3,512]{1,0:T(4,128)S(1)}, s32[3]{0:T(128)S(1)}, bf16[1536,768]{1,0:T(8,128)(2,1)}, /*index=5*/bf1...) while((s32[]{:T(128)}, f32[3,512]{1,0:T(4,128)S(1)}, ...), condition=%wide.region_9.11_spmd.clone, body=%wide.region_6.10_spmd.clone.sunk | while | flops 2422213120 | bytes 6338743 | solution.py:150
  550.1 9.5 %all-to-all-start.8 = ((f32[1,1,1,8,32,6]{3,2,5,1,0,4:T(1,128)}), f32[1,1,1,8,32,6]{3,2,5,1,0,4:T(1,128)S(1)}, u32[]{:S(2)}, u32[]{:S(2)}) async-start(f32[1,1,1,8,32,6]{3,2,5,1,0,4:T(1,128)} %copy.48), calls=%async_computation.8 | async-start | bytes 196608 | tf_op jit(solution)/shard_map/all_to_all | solution.py:166
  564.3 4.4 all-to-all-done.8
  570.7 5.3 all-to-all-start.9
  581.6 4.5 gather_fusion
  (101 shorter events, 97.4 us)
Async XLA Ops:
  7.2 24.2 %copy-start = (f32[768,768]{1,0:T(8,128)S(1)}, f32[768,768]{1,0:T(8,128)}, u32[]{:S(2)}) copy-start(f32[768,768]{1,0:T(8,128)} %param.7) | copy-start | bytes 7077892
  16.1 15.3 %copy-start.1 = (s32[1536]{0:T(1024)}, s32[1536]{0:T(1024)S(1)}, u32[]{:S(2)}) copy-start(s32[1536]{0:T(1024)S(1)} %scatter_custom_fusion.1) | copy-start | bytes 18436
  17.5 20.8 %all-to-all-start.6 = ((bf16[32,8,1,6]{3,1,2,0:T(8,128)(2,1)}), bf16[32,8,1,6]{3,1,2,0:T(8,128)(2,1)}, u32[]{:S(2)}, u32[]{:S(2)}) async-start(bf16[32,8,1,6]{3,1,2,0:T(8,128)(2,1)} %bitcast.11), calls=%async_computation.6 | async-start | bytes 131072 | tf_op jit(solution)/shard_map/all_to_all | solution.py:117
  38.3 17.6 %all-to-all-start.2 = ((bf16[32,8,1,6]{3,1,2,0:T(8,128)(2,1)}), bf16[32,8,1,6]{3,1,2,0:T(8,128)(2,1)}, u32[]{:S(2)}, u32[]{:S(2)}) async-start(bf16[32,8,1,6]{3,1,2,0:T(8,128)(2,1)} %bitcast.58), calls=%async_computation.2 | async-start | bytes 131072 | tf_op jit(solution)/shard_map/all_to_all | solution.py:108
  55.9 18.8 %all-to-all-start.7 = ((bf16[1,8,1,192]{3,2,0,1:T(2,128)(2,1)}), bf16[1,8,1,192]{3,2,0,1:T(2,128)(2,1)}, u32[]{:S(2)}, u32[]{:S(2)}) async-start(bf16[1,8,1,192]{3,2,0,1:T(2,128)(2,1)} %all_to_all.126), calls=%async_computation.7 | async-start | bytes 16384 | tf_op jit(solution)/shard_map/all_to_all | solution.py:116
  74.6 17.1 %all-to-all-start.3 = ((bf16[1,8,1,192]{3,2,0,1:T(2,128)(2,1)}), bf16[1,8,1,192]{3,2,0,1:T(2,128)(2,1)}, u32[]{:S(2)}, u32[]{:S(2)}) async-start(bf16[1,8,1,192]{3,2,0,1:T(2,128)(2,1)} %all_to_all.125), calls=%async_computation.3 | async-start | bytes 16384 | tf_op jit(solution)/shard_map/all_to_all | solution.py:107
  91.7 59.4 %all-to-all-start.4 = ((bf16[32,8,1,6,768]{4,1,3,2,0:T(8,128)(2,1)}), bf16[32,8,1,6,768]{4,1,3,2,0:T(8,128)(2,1)}, u32[]{:S(2)}, u32[]{:S(2)}) async-start(bf16[32,8,1,6,768]{4,1,3,2,0:T(8,128)(2,1)} %copy.42), calls=%async_computation.4 | async-start | bytes 4718592 | tf_op jit(solution)/shard_map/all_to_all | solution.py:99
  151.2 61.4 %all-to-all-start = ((bf16[32,8,1,6,768]{4,1,3,2,0:T(8,128)(2,1)}), bf16[32,8,1,6,768]{4,1,3,2,0:T(8,128)(2,1)}, u32[]{:S(2)}, u32[]{:S(2)}) async-start(bf16[32,8,1,6,768]{4,1,3,2,0:T(8,128)(2,1)} %copy.36), calls=%async_computation | async-start | bytes 4718592 | tf_op jit(solution)/shard_map/all_to_all | solution.py:90
  212.5 36.4 %all-to-all-start.5 = ((bf16[1,8,1,192,768]{4,3,2,0,1:T(8,128)(2,1)}), bf16[1,8,1,192,768]{4,3,2,0,1:T(8,128)(2,1)}, u32[]{:S(2)}, u32[]{:S(2)}) async-start(bf16[1,8,1,192,768]{4,3,2,0,1:T(8,128)(2,1)} %copy.43), calls=%async_computation.5 | async-start | bytes 4718592 | tf_op jit(solution)/shard_map/all_to_all | solution.py:98
  248.9 267.6 %all-to-all-start.1 = ((bf16[1,8,1,192,768]{4,3,2,0,1:T(8,128)(2,1)}), bf16[1,8,1,192,768]{4,3,2,0,1:T(8,128)(2,1)}, u32[]{:S(2)}, u32[]{:S(2)}) async-start(bf16[1,8,1,192,768]{4,3,2,0,1:T(8,128)(2,1)} %copy.37), calls=%async_computation.1 | async-start | bytes 4718592 | tf_op jit(solution)/shard_map/all_to_all | solution.py:89
  254.0 98.0 %copy-start.2 = (s32[768,1]{0,1:T(1,128)S(1)}, s32[768,1]{0,1:T(1,128)}, u32[]{:S(2)}) copy-start(s32[768,1]{0,1:T(1,128)} %param.8) | copy-start | bytes 9220
  254.0 261.2 %all-reduce.2.cloned.1.call-start = ((), (), s32[]{:S(2)}) async-start(), calls=%async_computation.10 | async-start | bytes 1572864 | tf_op jit(solution)/shard_map/psum | solution.py:73
  550.1 18.6 %all-to-all-start.8 = ((f32[1,1,1,8,32,6]{3,2,5,1,0,4:T(1,128)}), f32[1,1,1,8,32,6]{3,2,5,1,0,4:T(1,128)S(1)}, u32[]{:S(2)}, u32[]{:S(2)}) async-start(f32[1,1,1,8,32,6]{3,2,5,1,0,4:T(1,128)} %copy.48), calls=%async_computation.8 | async-start | bytes 196608 | tf_op jit(solution)/shard_map/all_to_all | solution.py:166
  570.7 9.9 %all-to-all-start.9 = ((f32[8,1,192]{2,1,0:T(1,128)}), f32[8,1,192]{2,1,0:T(1,128)S(1)}, u32[]{:S(2)}, u32[]{:S(2)}) async-start(f32[8,1,192]{2,1,0:T(1,128)} %reshape.394), calls=%async_computation.9 | async-start | bytes 16384 | tf_op jit(solution)/shard_map/all_to_all | solution.py:165
Sparse Core Ops, SparseCore 0:
  260.3 254.8 all-reduce.1
where the time goes:
time: 596 us; the launch traced here: 594 us
  waiting for transfers between devices  284 us (48%)
  blocking collectives  91.5 us (15%)
  starting transfers between devices  72.7 us (12%)
  local copies, waits for them, and re-layouts  68.2 us (11%)
  other arithmetic  34.3 us (6%)
  matrix products  23 us (4%)
  between operations  14.3 us (2%)
  loops' own time  5.96 us (1%)
    psum x1, waiting for transfers between devices, body(): lax.psum((cluster_sums, local_counts), ('corpus', 'group'))  161 us
    psum x1, blocking collectives, body(): lax.psum((cluster_sums, local_counts), ('corpus', 'group'))  91.5 us
    all_to_all x1, waiting for transfers between devices, body(): lax.all_to_all(member_buf.reshape(shape_rows), 'corpus', split_axis=0, co...  50.3 us
    all_to_all x1, waiting for transfers between devices, body(): lax.all_to_all(near_buf.reshape(shape_rows), 'corpus', split_axis=0, conc...  35.8 us
    all_to_all x1, waiting for transfers between devices, body(): lax.all_to_all(lax.all_to_all(near_buf.reshape(shape_rows), 'corpus', spl...  25.8 us
    dot_general x6, matrix products, pair_sums(): lax.dot_general(block_rows, col_rows, (((1,), (1,)), ((), ())), preferred...  21.4 us
    all_to_all x1, starting transfers between devices, body(): lax.all_to_all(near_mask.reshape(shape_mask), 'corpus', split_axis=0, con...  12 us
  transfers between devices with their start and end apart: 11, of which 8 were waited for; matrix products, arithmetic and copies ran while one was open for 13% of the time, Pallas kernels for 0%

commit v1 on v0

--- a/solution.py
+++ b/solution.py
@@ -1,3 +1,4 @@
+import functools
 import math
 import jax
 import jax.numpy as jnp
@@ -8,6 +9,15 @@
 SHARPNESS = 16.0
 TYPICAL_SCALE = 8.0
 EPSILON = 1e-06
+
+
+def see_the_knots(load, axis_tag, along_axis):
+    for u in (axis_tag, along_axis):
+        load = lax.psum(load, u)
+    return load
+
+
+wrap_map = functools.partial(see_the_knots, axis_tag="corpus", along_axis="group")
 
 
 def normalize(values):
@@ -70,7 +80,7 @@
         member_hot, unit_embed, (((0,), (0,)), ((), ())), preferred_element_type=jnp.float32
     )
     local_counts = jnp.sum(member_hot, axis=0, dtype=jnp.float32)
-    cluster_sums, counts = lax.psum((cluster_sums, local_counts), ("corpus", "group"))
+    cluster_sums, counts = wrap_map((cluster_sums, local_counts))
     centroid = normalize(cluster_sums)
     typical_rows = TYPICAL_SCALE * jnp.sum(
         unit_embed * jnp.take(centroid, row_label, axis=0), axis=1

time: 596 us -> 568 us (0.953)
  waiting for transfers between devices: 284 us -> 263 us
    psum x1 -> x2, waiting for transfers between devices: 161 us -> 141 us  [see_the_knots(): load = lax.psum(load, u)]
    psum x1 -> x2, blocking collectives: 91.5 us -> 89.5 us  [see_the_knots(): load = lax.psum(load, u)]
  transfers between devices with their start and end apart: 11 -> 12, of which waited for: 8 -> 8; matrix products, arithmetic and copies ran while one was open for 13% -> 13% of each run, Pallas kernels for 0% -> 0%
where the time goes in v1:
time: 568 us; the launch traced here: 566 us
  waiting for transfers between devices  263 us (46%)
  blocking collectives  89.5 us (16%)
  local copies, waits for them, and re-layouts  68.2 us (12%)
  starting transfers between devices  67.8 us (12%)
  other arithmetic  34.3 us (6%)
  matrix products  22.9 us (4%)
  between operations  14.3 us (3%)
  loops' own time  5.96 us (1%)
    psum x2, waiting for transfers between devices, see_the_knots(): load = lax.psum(load, u)  141 us
    psum x2, blocking collectives, see_the_knots(): load = lax.psum(load, u)  89.5 us
    all_to_all x1, waiting for transfers between devices, body(): lax.all_to_all(member_buf.reshape(shape_rows), 'corpus', split_axis=0, co...  50.3 us
    all_to_all x1, waiting for transfers between devices, body(): lax.all_to_all(near_buf.reshape(shape_rows), 'corpus', split_axis=0, conc...  35.8 us
    all_to_all x1, waiting for transfers between devices, body(): lax.all_to_all(lax.all_to_all(near_buf.reshape(shape_rows), 'corpus', spl...  25.8 us
    dot_general x6, matrix products, pair_sums(): lax.dot_general(block_rows, col_rows, (((1,), (1,)), ((), ())), preferred...  21.4 us
    all_to_all x1, starting transfers between devices, body(): lax.all_to_all(near_mask.reshape(shape_mask), 'corpus', split_axis=0, con...  12 us
    gather x2, local copies, waits for them, and re-layouts, fill_slots(): picked = jnp.take(unit_embed, jnp.maximum(source, 0), axis=0)  11.5 us
  transfers between devices with their start and end apart: 12, of which 8 were waited for; matrix products, arithmetic and copies ran while one was open for 13% of the time, Pallas kernels for 0%

profile of v1, /device:TPU:1, one launch (start us, length us, event | category | flops | bytes accessed | tf_op | source)
XLA Modules:
  0.0 565.9 jit_solution(15363117828954433257)
XLA Ops:
  17.5 12.0 %all-to-all-start.6 = ((bf16[32,8,1,6]{3,1,2,0:T(8,128)(2,1)}), bf16[32,8,1,6]{3,1,2,0:T(8,128)(2,1)}, u32[]{:S(2)}, u32[]{:S(2)}) async-start(bf16[32,8,1,6]{3,1,2,0:T(8,128)(2,1)} %bitcast.11), calls=%async_computation.6 | async-start | bytes 131072 | tf_op jit(solution)/shard_map/all_to_all | solution.py:127
  38.3 8.8 %all-to-all-start.2 = ((bf16[32,8,1,6]{3,1,2,0:T(8,128)(2,1)}), bf16[32,8,1,6]{3,1,2,0:T(8,128)(2,1)}, u32[]{:S(2)}, u32[]{:S(2)}) async-start(bf16[32,8,1,6]{3,1,2,0:T(8,128)(2,1)} %bitcast.58), calls=%async_computation.2 | async-start | bytes 131072 | tf_op jit(solution)/shard_map/all_to_all | solution.py:118
  55.9 7.1 %all-to-all-start.7 = ((bf16[1,8,1,192]{3,2,0,1:T(2,128)(2,1)}), bf16[1,8,1,192]{3,2,0,1:T(2,128)(2,1)}, u32[]{:S(2)}, u32[]{:S(2)}) async-start(bf16[1,8,1,192]{3,2,0,1:T(2,128)(2,1)} %all_to_all.126), calls=%async_computation.7 | async-start | bytes 16384 | tf_op jit(solution)/shard_map/all_to_all | solution.py:126
  64.3 5.7 %gather_fusion.3 = bf16[1536,768]{1,0:T(8,128)(2,1)} fusion(bf16[768,768]{1,0:T(8,128)(2,1)S(1)} %multiply_convert_fusion, s32[2048]{0:T(1024)} %pad_clamp_fusion), kind=kCustom, calls=%fused_computation.1.clone | custom fusion | bytes 4724736 | tf_op jit(solution)/shard_map/jit(_take)/gather | solution.py:39
  74.6 4.8 all-to-all-start.3
  82.8 5.0 reshape.320
  91.7 5.5 all-to-all-start.4
  97.2 5.7 %gather_fusion.2 = bf16[1536,768]{1,0:T(8,128)(2,1)} fusion(bf16[768,768]{1,0:T(8,128)(2,1)S(1)} %multiply_convert_fusion, s32[2048]{0:T(1024)S(1)} %pad_clamp_fusion.1), kind=kCustom, calls=%fused_computation.clone | custom fusion | bytes 4724736 | tf_op jit(solution)/shard_map/jit(_take)/gather | solution.py:39
  106.3 5.0 reshape.317
  111.4 3.9 copy.36
  115.3 35.8 %all-to-all-done.4 = bf16[32,8,1,6,768]{4,1,3,2,0:T(8,128)(2,1)} async-done(((bf16[32,8,1,6,768]{4,1,3,2,0:T(8,128)(2,1)}), bf16[32,8,1,6,768]{4,1,3,2,0:T(8,128)(2,1)}, u32[]{:S(2)}, u32[]{:S(2)}) %all-to-all-start.4) | async-done | bytes 2359328 | tf_op jit(solution)/shard_map/all_to_all | solution.py:109
  151.2 7.6 %all-to-all-start = ((bf16[32,8,1,6,768]{4,1,3,2,0:T(8,128)(2,1)}), bf16[32,8,1,6,768]{4,1,3,2,0:T(8,128)(2,1)}, u32[]{:S(2)}, u32[]{:S(2)}) async-start(bf16[32,8,1,6,768]{4,1,3,2,0:T(8,128)(2,1)} %copy.36), calls=%async_computation | async-start | bytes 4718592 | tf_op jit(solution)/shard_map/all_to_all | solution.py:100
  162.2 50.3 %all-to-all-done = bf16[32,8,1,6,768]{4,1,3,2,0:T(8,128)(2,1)} async-done(((bf16[32,8,1,6,768]{4,1,3,2,0:T(8,128)(2,1)}), bf16[32,8,1,6,768]{4,1,3,2,0:T(8,128)(2,1)}, u32[]{:S(2)}, u32[]{:S(2)}) %all-to-all-start) | async-done | bytes 2359328 | tf_op jit(solution)/shard_map/all_to_all | solution.py:100
  212.5 7.1 %all-to-all-start.5 = ((bf16[1,8,1,192,768]{4,3,2,0,1:T(8,128)(2,1)}), bf16[1,8,1,192,768]{4,3,2,0,1:T(8,128)(2,1)}, u32[]{:S(2)}, u32[]{:S(2)}) async-start(bf16[1,8,1,192,768]{4,3,2,0,1:T(8,128)(2,1)} %copy.43), calls=%async_computation.5 | async-start | bytes 4718592 | tf_op jit(solution)/shard_map/all_to_all | solution.py:108
  223.1 25.8 %all-to-all-done.5 = bf16[1,8,1,192,768]{4,3,2,0,1:T(8,128)(2,1)} async-done(((bf16[1,8,1,192,768]{4,3,2,0,1:T(8,128)(2,1)}), bf16[1,8,1,192,768]{4,3,2,0,1:T(8,128)(2,1)}, u32[]{:S(2)}, u32[]{:S(2)}) %all-to-all-start.5) | async-done | bytes 2359328 | tf_op jit(solution)/shard_map/all_to_all | solution.py:108
  248.9 5.1 all-to-all-start.1
  258.5 140.9 %all-reduce.3.cloned.1.call-done = f32[256,768]{1,0:T(8,128)} async-done(((f32[256,768]{1,0:T(8,128)}), f32[256,768]{1,0:T(8,128)}) %all-reduce.3.cloned.1.call-update) | async-done | bytes 786448 | tf_op jit(solution)/shard_map/psum | solution.py:16
  399.4 59.4 %psum.28 = f32[256]{0:T(256)S(1)} all-reduce(f32[256]{0:T(256)S(1)} %convert_reduce_fusion.1), channel_id=1, replica_groups=mesh['corpus'=32,'group'=8] {'corpus'}, use_global_device_ids=true, to_apply=%region_11.13 | all-reduce | flops 256 | bytes 2048 | tf_op jit(solution)/shard_map/psum | solution.py:16
  458.8 30.0 %psum.29 = f32[256]{0:T(256)S(1)} all-reduce(f32[256]{0:T(256)S(1)} %psum.28), channel_id=1, replica_groups=mesh['corpus'=32,'group'=8] {'group'}, use_global_device_ids=true, to_apply=%region_12.14 | all-reduce | flops 256 | bytes 2048 | tf_op jit(solution)/shard_map/psum | solution.py:16
  493.8 31.4 %while.21 = (s32[]{:T(128)}, f32[3,512]{1,0:T(4,128)S(1)}, f32[3,512]{1,0:T(4,128)S(1)}, s32[3]{0:T(128)S(1)}, bf16[1536,768]{1,0:T(8,128)(2,1)}, /*index=5*/bf1...) while((s32[]{:T(128)}, f32[3,512]{1,0:T(4,128)S(1)}, ...), condition=%wide.region_9.11_spmd.clone, body=%wide.region_6.10_spmd.clone.sunk | while | flops 2422213120 | bytes 6338743 | solution.py:160
  527.4 4.6 all-to-all-start.8
  536.7 4.4 all-to-all-done.8
  543.1 5.2 all-to-all-start.9
  554.0 4.5 gather_fusion
  (105 shorter events, 101.3 us)
Async XLA Ops:
  7.2 24.2 %copy-start = (f32[768,768]{1,0:T(8,128)S(1)}, f32[768,768]{1,0:T(8,128)}, u32[]{:S(2)}) copy-start(f32[768,768]{1,0:T(8,128)} %param.7) | copy-start | bytes 7077892
  16.1 15.3 %copy-start.1 = (s32[1536]{0:T(1024)}, s32[1536]{0:T(1024)S(1)}, u32[]{:S(2)}) copy-start(s32[1536]{0:T(1024)S(1)} %scatter_custom_fusion.1) | copy-start | bytes 18436
  17.5 20.8 %all-to-all-start.6 = ((bf16[32,8,1,6]{3,1,2,0:T(8,128)(2,1)}), bf16[32,8,1,6]{3,1,2,0:T(8,128)(2,1)}, u32[]{:S(2)}, u32[]{:S(2)}) async-start(bf16[32,8,1,6]{3,1,2,0:T(8,128)(2,1)} %bitcast.11), calls=%async_computation.6 | async-start | bytes 131072 | tf_op jit(solution)/shard_map/all_to_all | solution.py:127
  38.3 17.6 %all-to-all-start.2 = ((bf16[32,8,1,6]{3,1,2,0:T(8,128)(2,1)}), bf16[32,8,1,6]{3,1,2,0:T(8,128)(2,1)}, u32[]{:S(2)}, u32[]{:S(2)}) async-start(bf16[32,8,1,6]{3,1,2,0:T(8,128)(2,1)} %bitcast.58), calls=%async_computation.2 | async-start | bytes 131072 | tf_op jit(solution)/shard_map/all_to_all | solution.py:118
  55.9 18.8 %all-to-all-start.7 = ((bf16[1,8,1,192]{3,2,0,1:T(2,128)(2,1)}), bf16[1,8,1,192]{3,2,0,1:T(2,128)(2,1)}, u32[]{:S(2)}, u32[]{:S(2)}) async-start(bf16[1,8,1,192]{3,2,0,1:T(2,128)(2,1)} %all_to_all.126), calls=%async_computation.7 | async-start | bytes 16384 | tf_op jit(solution)/shard_map/all_to_all | solution.py:126
  74.6 17.1 %all-to-all-start.3 = ((bf16[1,8,1,192]{3,2,0,1:T(2,128)(2,1)}), bf16[1,8,1,192]{3,2,0,1:T(2,128)(2,1)}, u32[]{:S(2)}, u32[]{:S(2)}) async-start(bf16[1,8,1,192]{3,2,0,1:T(2,128)(2,1)} %all_to_all.125), calls=%async_computation.3 | async-start | bytes 16384 | tf_op jit(solution)/shard_map/all_to_all | solution.py:117
  91.7 59.4 %all-to-all-start.4 = ((bf16[32,8,1,6,768]{4,1,3,2,0:T(8,128)(2,1)}), bf16[32,8,1,6,768]{4,1,3,2,0:T(8,128)(2,1)}, u32[]{:S(2)}, u32[]{:S(2)}) async-start(bf16[32,8,1,6,768]{4,1,3,2,0:T(8,128)(2,1)} %copy.42), calls=%async_computation.4 | async-start | bytes 4718592 | tf_op jit(solution)/shard_map/all_to_all | solution.py:109
  151.2 61.4 %all-to-all-start = ((bf16[32,8,1,6,768]{4,1,3,2,0:T(8,128)(2,1)}), bf16[32,8,1,6,768]{4,1,3,2,0:T(8,128)(2,1)}, u32[]{:S(2)}, u32[]{:S(2)}) async-start(bf16[32,8,1,6,768]{4,1,3,2,0:T(8,128)(2,1)} %copy.36), calls=%async_computation | async-start | bytes 4718592 | tf_op jit(solution)/shard_map/all_to_all | solution.py:100
  212.5 36.4 %all-to-all-start.5 = ((bf16[1,8,1,192,768]{4,3,2,0,1:T(8,128)(2,1)}), bf16[1,8,1,192,768]{4,3,2,0,1:T(8,128)(2,1)}, u32[]{:S(2)}, u32[]{:S(2)}) async-start(bf16[1,8,1,192,768]{4,3,2,0,1:T(8,128)(2,1)} %copy.43), calls=%async_computation.5 | async-start | bytes 4718592 | tf_op jit(solution)/shard_map/all_to_all | solution.py:108
  248.9 244.9 %all-to-all-start.1 = ((bf16[1,8,1,192,768]{4,3,2,0,1:T(8,128)(2,1)}), bf16[1,8,1,192,768]{4,3,2,0,1:T(8,128)(2,1)}, u32[]{:S(2)}, u32[]{:S(2)}) async-start(bf16[1,8,1,192,768]{4,3,2,0,1:T(8,128)(2,1)} %copy.37), calls=%async_computation.1 | async-start | bytes 4718592 | tf_op jit(solution)/shard_map/all_to_all | solution.py:99
  254.0 236.8 %copy-start.2 = (s32[768,1]{0,1:T(1,128)S(1)}, s32[768,1]{0,1:T(1,128)}, u32[]{:S(2)}) copy-start(s32[768,1]{0,1:T(1,128)} %param.8) | copy-start | bytes 9220
  254.0 145.4 %all-reduce.3.cloned.1.call-start = ((), (), s32[]{:S(2)}) async-start(), calls=%async_computation.10 | async-start | bytes 1572864 | tf_op jit(solution)/shard_map/psum | solution.py:16
  255.6 237.0 %all-reduce.5.cloned.1.call-start = ((), (), s32[]{:S(2)}) async-start(), calls=%async_computation.11 | async-start | bytes 1572864 | tf_op jit(solution)/shard_map/psum | solution.py:16
  527.4 13.7 %all-to-all-start.8 = ((f32[1,1,1,8,32,6]{3,2,5,1,0,4:T(1,128)}), f32[1,1,1,8,32,6]{3,2,5,1,0,4:T(1,128)S(1)}, u32[]{:S(2)}, u32[]{:S(2)}) async-start(f32[1,1,1,8,32,6]{3,2,5,1,0,4:T(1,128)} %copy.48), calls=%async_computation.8 | async-start | bytes 196608 | tf_op jit(solution)/shard_map/all_to_all | solution.py:176
  543.1 9.8 %all-to-all-start.9 = ((f32[8,1,192]{2,1,0:T(1,128)}), f32[8,1,192]{2,1,0:T(1,128)S(1)}, u32[]{:S(2)}, u32[]{:S(2)}) async-start(f32[8,1,192]{2,1,0:T(1,128)} %reshape.394), calls=%async_computation.9 | async-start | bytes 16384 | tf_op jit(solution)/shard_map/all_to_all | solution.py:175
Sparse Core Ops, SparseCore 0:
  258.2 141.1 all-reduce.2
  401.7 66.9 all-reduce.4
